TPU v7x, 512 devices: a whole 4x4x16 slice. The times are simulated.
512 devices in a mesh: tok: 64 (over z, x), head: 8 (over y, core).
Axes of the slice: x: 4, y: 4, z: 16, core: 2. Of those that a mesh axis runs over, the one named last changes fastest.
Arguments:
- tokens: bfloat16 [32768, 2560], P('tok', 'head'), may hold values from -6 to 6
- query_weight: bfloat16 [2560, 2560], P('tok'), may hold values from -0.125 to 0.125
- keyvalue_weight: bfloat16 [2560, 512], P('tok'), may hold values from -0.125 to 0.125
- output_weight: bfloat16 [2560, 2560], P(None, ('head', 'tok')), may hold values from -0.125 to 0.125
- cache: bfloat16 [2048, 2, 128, 256], P(('tok', 'head')), may hold values from -460 to 460
- page_table: int32 [512, 4], P('tok'), may hold values from 0 to 2047, as said below
- parents: int32 [512, 64], P('tok'), may hold values from 0 to 62, as said below
- cache_len: int32 [512], P('tok'), may hold values from 1 to 448, as said below
- accepted_leaf: int32 [512], P('tok'), may hold values from 0 to 63
Outputs:
- attended: bfloat16 [32768, 2560], P('tok', 'head')
- cache_out: bfloat16 [2048, 2, 128, 256], P(('tok', 'head'))
Inputs may be any that keep to these rules, and one draw needn't show every extreme that they name: `page_table`: for every d, row d names each of the pages d * 4 to d * 4 + 3 exactly once, so request d's pages all lie on device d (devices counted tok-major, head-minor). parents[r, 0] = 0, and parents[r, i] < i for i >= 1. `cache_len`: roughly half of the requests hold at most 128 cached positions, the others more than 320.
All inputs are finite; a program needn't handle non-finite values.
Results may differ from a plain program's by a relative error of at most 0.014.
The roundings to bfloat16 on the way count: a program that leaves them out, or rounds other values in their place, can miss the bound.
Values may be sent and summed in bfloat16 or wider, within the bound.
No kernel may reach another device: no remote copies, remote signals or barrier semaphores. Data moves between devices by JAX's collectives and lax.ppermute only.
A program may use at most 64 MiB of HBM per device.

v0:
```python
import math
import jax
import jax.numpy as jnp
from jax import lax
from jax.sharding import PartitionSpec as P

HQ = 10
HD = 256
DRAFT = 64
PAGE = 128
NPR = 4
WINDOW = 256


def ancestry(parent_row):
    node_ids = jnp.arange(DRAFT, dtype=jnp.int32)
    link = (parent_row[:, None] == node_ids[None, :]).astype(jnp.float32)
    reach = jnp.minimum(link + jnp.eye(DRAFT, dtype=jnp.float32), 1.0)
    for sweep in range((DRAFT - 1).bit_length()):
        reach = jnp.minimum(jnp.dot(reach, reach, precision=lax.Precision.HIGHEST), 1.0)
    depth = (jnp.sum(reach, axis=1) - 1.0).astype(jnp.int32)
    return (reach, depth)


def rotate(values, position):
    half = HD // 4
    freq = jnp.exp(jnp.arange(half, dtype=jnp.float32) * (-2.0 * math.log(10000.0) / (HD // 2)))
    angle = position.astype(jnp.float32)[..., None] * freq
    cosine = jnp.cos(angle)
    sine = jnp.sin(angle)
    first = values[..., :half]
    second = values[..., half : 2 * half]
    return jnp.concatenate(
        [first * cosine - second * sine, second * cosine + first * sine, values[..., 2 * half :]],
        axis=-1,
    )


def attend(queries, cache_keys, cache_values, tree_keys, tree_values, lengths, position, reach):
    window_span = cache_keys.shape[1]
    slot_ids = jnp.arange(window_span, dtype=jnp.int32)
    visible = (slot_ids[None, None, :] < lengths[:, None, None]) & (
        slot_ids[None, None, :] > position[:, :, None] - WINDOW
    )
    cache_scores = jnp.einsum(
        "rnhd,rcd->rhnc", queries, cache_keys, preferred_element_type=jnp.float32
    )
    tree_scores = jnp.einsum(
        "rnhd,rmd->rhnm", queries, tree_keys, preferred_element_type=jnp.float32
    )
    cache_scores = jnp.where(visible[:, None], cache_scores, -1e30)
    tree_scores = jnp.where(reach[:, None] > 0.5, tree_scores, -1e30)
    row_peak = jnp.maximum(jnp.max(cache_scores, axis=-1), jnp.max(tree_scores, axis=-1))[..., None]
    cache_weights = jnp.exp(cache_scores - row_peak)
    tree_weights = jnp.exp(tree_scores - row_peak)
    denominator = jnp.sum(cache_weights, axis=-1, keepdims=True) + jnp.sum(
        tree_weights, axis=-1, keepdims=True
    )
    cache_weights = (cache_weights / denominator).astype(jnp.bfloat16)
    tree_weights = (tree_weights / denominator).astype(jnp.bfloat16)
    result = jnp.einsum(
        "rhnc,rcd->rnhd", cache_weights, cache_values, preferred_element_type=jnp.float32
    )
    result = result + jnp.einsum(
        "rhnm,rmd->rnhd", tree_weights, tree_values, preferred_element_type=jnp.float32
    )
    return result.astype(jnp.bfloat16)


def refresh(logical_pages, length, leaf, reach, depth, new_keys, new_values):
    count = logical_pages.shape[0] * logical_pages.shape[2]
    logical = jnp.transpose(logical_pages, (1, 0, 2, 3)).reshape(2, count, HD)
    slot_ids = jnp.arange(count, dtype=jnp.int32)
    on_path = reach[leaf]
    selector = ((on_path[None, :] > 0.5) & (depth[None, :] == slot_ids[:, None] - length)).astype(
        jnp.float32
    )
    placed_keys = jnp.dot(selector, new_keys.astype(jnp.float32), precision=lax.Precision.HIGHEST)
    placed_values = jnp.dot(
        selector, new_values.astype(jnp.float32), precision=lax.Precision.HIGHEST
    )
    placed = jnp.stack([placed_keys, placed_values]).astype(jnp.bfloat16)
    written = jnp.sum(selector, axis=1) > 0.5
    logical = jnp.where(written[None, :, None], placed, logical)
    return jnp.transpose(
        logical.reshape(2, logical_pages.shape[0], logical_pages.shape[2], HD), (1, 0, 2, 3)
    )


def shards(
    tokens,
    query_weight,
    keyvalue_weight,
    output_weight,
    cache,
    page_table,
    parents,
    cache_len,
    accepted_leaf,
):
    head_count = lax.axis_size("head")
    head_index = lax.axis_index("head")
    tok_index = lax.axis_index("tok")
    requests = parents.shape[0]
    assert requests == head_count
    pages_dev = cache.shape[0]
    part_rows = query_weight.shape[0]
    q_cols = HQ * HD // head_count
    kv_cols = 2 * HD // head_count
    out_cols = output_weight.shape[1]
    wq_piece = lax.dynamic_slice_in_dim(query_weight, head_index * q_cols, q_cols, axis=1)
    wkv_piece = lax.dynamic_slice_in_dim(keyvalue_weight, head_index * kv_cols, kv_cols, axis=1)
    flat = jnp.concatenate([wq_piece.reshape(-1), wkv_piece.reshape(-1), output_weight.reshape(-1)])
    stacked = lax.all_gather(flat, "tok", axis=0, tiled=False)
    tok_count = stacked.shape[0]
    n_q = part_rows * q_cols
    n_kv = part_rows * kv_cols
    wq_cols = stacked[:, :n_q].reshape(tok_count * part_rows, q_cols)
    wkv_cols = stacked[:, n_q : n_q + n_kv].reshape(tok_count * part_rows, kv_cols)
    wo_cols = (
        stacked[:, n_q + n_kv :]
        .reshape(tok_count, HQ * HD, out_cols)
        .transpose(1, 0, 2)
        .reshape(HQ * HD, tok_count * out_cols)
    )
    gathered = lax.all_gather(tokens, "head", axis=1, tiled=True)
    wide = gathered.astype(jnp.float32)
    mean_square = jnp.mean(wide * wide, axis=1, keepdims=True)
    normed = (wide * lax.rsqrt(mean_square + 1e-06)).astype(jnp.bfloat16)
    q_part = jnp.dot(normed, wq_cols, preferred_element_type=jnp.float32)
    kv_part = jnp.dot(normed, wkv_cols, preferred_element_type=jnp.float32)
    both = jnp.concatenate([q_part, kv_part], axis=1)
    mine = lax.all_to_all(both, "head", 0, 1, tiled=True)
    mine = mine.reshape(DRAFT, head_count, q_cols + kv_cols)
    q_pre = mine[:, :, :q_cols].reshape(DRAFT, HQ, HD)
    kv_pre = mine[:, :, q_cols:].reshape(DRAFT, 2 * HD)
    parent_row = lax.dynamic_index_in_dim(parents, head_index, 0, keepdims=False)
    length = lax.dynamic_index_in_dim(cache_len, head_index, 0, keepdims=False)
    leaf = lax.dynamic_index_in_dim(accepted_leaf, head_index, 0, keepdims=False)
    reach, depth = ancestry(parent_row)
    position = length + depth
    queries = (rotate(q_pre, position[:, None]) * HD ** (-0.5)).astype(jnp.bfloat16)
    tree_keys = rotate(kv_pre[:, :HD], position).astype(jnp.bfloat16)
    tree_values = kv_pre[:, HD:].astype(jnp.bfloat16)
    device = tok_index * head_count + head_index
    own_table = (
        lax.dynamic_index_in_dim(page_table, head_index, 0, keepdims=False) - device * pages_dev
    )
    own_pages = jnp.take(cache, own_table, axis=0)
    cache_keys = own_pages[:, 0].reshape(NPR * PAGE, HD)
    cache_values = own_pages[:, 1].reshape(NPR * PAGE, HD)
    result = attend(
        queries[None],
        cache_keys[None],
        cache_values[None],
        tree_keys[None],
        tree_values[None],
        length[None],
        position[None],
        reach[None],
    )
    mixed = lax.all_gather(result.reshape(DRAFT, HQ * HD), "head", axis=0, tiled=True)
    summed = jnp.zeros((mixed.shape[0], wo_cols.shape[1]), jnp.float32)
    for group in range(head_count):
        head_ids = [k for k in range(group, HQ, head_count)]
        if not head_ids:
            continue
        columns = jnp.concatenate([mixed[:, k * HD : (k + 1) * HD] for k in head_ids], axis=1)
        rows = jnp.concatenate([wo_cols[k * HD : (k + 1) * HD] for k in head_ids], axis=0)
        partial_value = jnp.dot(columns, rows, preferred_element_type=jnp.float32)
        summed = summed + partial_value.astype(jnp.bfloat16).astype(jnp.float32)
    attended = summed.astype(jnp.bfloat16)
    new_pages = refresh(own_pages, length, leaf, reach, depth, tree_keys, tree_values)
    matches = (own_table[:, None] == jnp.arange(pages_dev, dtype=jnp.int32)[None, :]).astype(
        jnp.int32
    )
    inverse = jnp.sum(matches * jnp.arange(pages_dev, dtype=jnp.int32)[:, None], axis=0)
    cache_out = jnp.take(new_pages, inverse, axis=0)
    return (attended, cache_out)


def solution(mesh):
    in_specs = (
        P("tok", "head"),
        P("tok", None),
        P("tok", None),
        P(None, ("head", "tok")),
        P(("tok", "head"), None, None, None),
        P("tok", None),
        P("tok", None),
        P("tok"),
        P("tok"),
    )
    out_specs = (P("tok", "head"), P(("tok", "head"), None, None, None))
    return jax.shard_map(shards, mesh=mesh, in_specs=in_specs, out_specs=out_specs, check_vma=False)
```

profile of v0, /device:TPU:1, one launch (start us, length us, event | category | flops | bytes accessed | tf_op | source)
XLA Modules:
  0.0 285.6 jit_solution(11939136876773440064)
XLA Ops:
  7.2 0.7 all-gather.6.cloned.1.call-update
  8.0 0.9 constant_dynamic-slice_fusion.2
  9.0 0.8 constant_dynamic-slice_fusion.1
  9.8 1.2 copy.62
  11.0 1.0 reshape.334
  12.0 0.7 reshape.362
  12.7 1.3 dynamic_slice.29
  15.4 1.2 dynamic_slice.25
  16.7 0.7 fusion.70
  19.5 0.7 iota_subtract_fusion
  20.4 29.1 %all-gather.6.cloned.1.call-done = bf16[512,2560]{0,1:T(8,128)(2,1)} async-done(((bf16[512,320]{0,1:T(8,128)(2,1)}), bf16[512,2560]{0,1:T(8,128)(2,1)}) %all-gather.6.cloned.1.call-update) | async-done | bytes 2621456 | tf_op jit(solution)/shard_map/all_gather | solution.py:126
  49.5 2.4 fusion
  51.9 146.4 %all-gather.10.cloned.1.call-done = bf16[64,1,28160]{2,1,0:T(2,128)(2,1)} async-done(((bf16[1,1,28160]{2,1,0:T(2,128)(2,1)}), bf16[64,1,28160]{2,1,0:T(2,128)(2,1)}) %all-gather.10.cloned.1.call-update) | async-done | bytes 3604496 | tf_op jit(solution)/shard_map/all_gather | solution.py:114
  198.3 3.5 %copy.97 = bf16[64,1,28160]{2,0,1:T(8,128)(2,1)S(1)} copy(bf16[64,1,28160]{2,1,0:T(2,128)(2,1)} %all-gather.10.cloned.1.call-done) | data formatting | bytes 7208960
  201.7 1.4 fusion.79
  203.1 2.5 reshape.335
  205.6 0.4 reshape.336
  206.0 3.6 %fusion.4 = f32[512,320]{0,1:T(8,128)S(1)} fusion(bf16[2560,320]{1,0:T(8,128)(2,1)} %reshape.335, bf16[512,2560]{0,1:T(8,128)(2,1)} %all-gather.6.cloned.1.call-done, f32[512]{0:T(512)S(1)} %add_rsqrt_fusion), kind=kOutput, calls=%fused_computation.8 | convolution fusion | flops 842792960 | bytes 4917248 | tf_op jit(solution)/shard_map/dot_general | solution.py:130
  209.7 0.7 fusion.2
  210.5 1.2 copy.63
  211.6 12.7 %all-to-all-start = ((f32[8,64,384]{2,1,0:T(8,128)}), f32[8,64,384]{2,1,0:T(8,128)S(1)}, u32[]{:S(2)}, u32[]{:S(2)}) async-start(f32[8,64,384]{2,1,0:T(8,128)} %bitcast.6), calls=%async_computation | async-start | bytes 1572864 | tf_op jit(solution)/shard_map/all_to_all | solution.py:133
  224.3 0.6 iota_compare_fusion.6
  225.1 0.6 gather_fusion
  225.7 0.7 add_add_fusion
  226.4 10.0 %all-to-all-done = f32[8,64,384]{2,1,0:T(8,128)S(1)} async-done(((f32[8,64,384]{2,1,0:T(8,128)}), f32[8,64,384]{2,1,0:T(8,128)S(1)}, u32[]{:S(2)}, u32[]{:S(2)}) %all-to-all-start) | async-done | bytes 786464 | tf_op jit(solution)/shard_map/all_to_all | solution.py:133
  236.9 0.3 convolution_convert_fusion.8
  237.3 0.5 copy.64
  237.7 0.4 reshape.337
  238.6 0.3 convolution_convert_fusion.9
  239.0 1.0 fusion.36
  240.3 0.4 fusion.84
  240.7 0.5 fusion.83
  241.3 0.4 fusion.26
  241.7 0.3 fusion.50
  242.0 0.4 fusion.85
  242.5 0.7 copy.90
  243.5 2.9 %copy.72 = bf16[64,12800]{0,1:T(8,128)(2,1)} copy(bf16[64,12800]{1,0:T(8,128)(2,1)S(1)} %copy-done.1) | data formatting | bytes 3276800 | tf_op jit(solution)/shard_map/slice | solution.py:121
  246.4 7.1 %reshape.342 = bf16[64,2560,5]{0,2,1:T(8,128)(2,1)} reshape(bf16[64,12800]{0,1:T(8,128)(2,1)} %copy.72) | data formatting | bytes 3276800 | tf_op jit(solution)/shard_map/reshape | solution.py:122
  253.5 4.9 %fusion.78 = (bf16[256,64,5]{1,2,0:T(8,128)(2,1)S(1)}, bf16[256,64,5]{1,2,0:T(8,128)(2,1)S(1)}, bf16[256,64,5]{1,2,0:T(8,128)(2,1)S(1)}, bf16[256,64,5]{1,2,0:T(...) fusion(bf16[2560,64,5]{1,2,0:T(8,128)(2,1)} %bitcast.112), kind=kLoop, calls=%fused_computation.143 | loop fusion | bytes 3276800 | tf_op jit(solution)/shard_map/slice | solution.py:169
  258.4 1.5 copy.73
  259.9 0.7 slice.155
  260.7 1.5 copy.74
  262.1 0.7 slice.157
  262.9 1.5 copy.75
  264.4 0.7 slice.161
  265.1 1.5 copy.76
  266.6 0.7 slice.163
  267.4 1.5 copy.77
  268.9 0.7 slice.166
  269.6 0.4 copy.78
  270.0 0.7 slice.169
  270.8 0.4 copy.79
  271.3 0.4 copy.80
  271.8 0.4 copy.81
  272.4 0.4 copy.82
  272.9 0.6 gather_fusion.1
  273.5 0.9 broadcast_select_fusion
  274.4 1.4 fusion.80
  275.9 0.4 fusion.23
  276.3 0.4 fusion.22
  277.2 0.3 fusion.16
  277.5 0.3 fusion.14
  277.8 0.3 fusion.12
  278.1 1.0 fusion.10
  (77 shorter events, 4.6 us)
Async XLA Ops:
  7.2 217.9 %copy-start = (bf16[4,2,128,256]{3,2,1,0:T(8,128)(2,1)S(1)}, bf16[4,2,128,256]{3,2,1,0:T(8,128)(2,1)}, u32[]{:S(2)}) copy-start(bf16[4,2,128,256]{3,2,1,0:T(8,128)(2,1)} %param.15) | copy-start | bytes 1572868
  7.2 12.1 %copy-start.11 = (s32[8,4]{0,1:T(4,128)S(1)}, s32[8,4]{0,1:T(4,128)}, u32[]{:S(2)}) copy-start(s32[8,4]{0,1:T(4,128)} %param.16) | copy-start | bytes 388
  7.2 42.3 %all-gather.6.cloned.1.call-start = ((), (), s32[]{:S(2)}) async-start(), calls=%async_computation.1 | async-start | bytes 2949120 | tf_op jit(solution)/shard_map/all_gather | solution.py:126
  7.9 190.3 %all-gather.10.cloned.1.call-start = ((), (), s32[]{:S(2)}) async-start(), calls=%async_computation.3 | async-start | bytes 7321600 | tf_op jit(solution)/shard_map/all_gather | solution.py:114
  206.0 3.7 %copy-start.2 = (bf16[512,2560]{0,1:T(8,128)(2,1)S(1)}, bf16[512,2560]{0,1:T(8,128)(2,1)}, u32[]{:S(2)}) copy-start(bf16[512,2560]{0,1:T(8,128)(2,1)} %all-gather.6.cloned.1.call-done) | copy-start | bytes 7864324
  211.6 24.9 %all-to-all-start = ((f32[8,64,384]{2,1,0:T(8,128)}), f32[8,64,384]{2,1,0:T(8,128)S(1)}, u32[]{:S(2)}, u32[]{:S(2)}) async-start(f32[8,64,384]{2,1,0:T(8,128)} %bitcast.6), calls=%async_computation | async-start | bytes 1572864 | tf_op jit(solution)/shard_map/all_to_all | solution.py:133
  224.3 50.1 %all-gather.8.cloned.1.call-start = ((), (), s32[]{:S(2)}) async-start(), calls=%async_computation.2 | async-start | bytes 2949120 | tf_op jit(solution)/shard_map/all_gather | solution.py:162
  242.0 1.5 copy-start.1
  270.0 2.9 %copy-start.4 = (bf16[4,2,128,256]{3,2,1,0:T(8,128)(2,1)S(1)}, bf16[4,2,128,256]{3,2,1,0:T(8,128)(2,1)}, u32[]{:S(2)}) copy-start(bf16[4,2,128,256]{3,2,1,0:T(8,128)(2,1)} %get-tuple-element.3) | copy-start | bytes 1572868
  272.3 3.5 %copy-start.9 = (bf16[256,320]{0,1:T(8,128)(2,1)S(1)}, bf16[256,320]{0,1:T(8,128)(2,1)}, u32[]{:S(2)}) copy-start(bf16[256,320]{0,1:T(8,128)(2,1)} %slice.155) | copy-start | bytes 491524
  272.4 3.5 %copy-start.10 = (bf16[256,320]{0,1:T(8,128)(2,1)S(1)}, bf16[256,320]{0,1:T(8,128)(2,1)}, u32[]{:S(2)}) copy-start(bf16[256,320]{0,1:T(8,128)(2,1)} %slice.157) | copy-start | bytes 491524
  273.5 2.8 copy-start.5
  273.5 2.8 copy-start.6
  274.4 2.2 copy-start.7
  274.4 2.2 copy-start.3
  275.9 1.1 copy-start.8
Sparse Core Ops, SparseCore 0:
  10.1 39.3 all-gather.5
  53.1 145.1 all-gather.9
  243.4 27.9 all-gather.7
where the time goes:
time: 287 us; the launch traced here: 286 us
  waiting for transfers between devices  186 us (65%)
  local copies, waits for them, and re-layouts  51.5 us (18%)
  between operations  16.5 us (6%)
  starting transfers between devices  12.8 us (4%)
  matrix products  10.8 us (4%)
  other arithmetic  7.81 us (3%)
    all_gather x1, waiting for transfers between devices, shards(): stacked = lax.all_gather(flat, 'tok', axis=0, tiled=False)  146 us
    all_gather x1, waiting for transfers between devices, shards(): gathered = lax.all_gather(tokens, 'head', axis=1, tiled=True)  29.1 us
    slice x21, local copies, waits for them, and re-layouts, shards(): wo_cols[k * HD:(k + 1) * HD]  19.2 us
    all_to_all x1, starting transfers between devices, shards(): mine = lax.all_to_all(both, 'head', 0, 1, tiled=True)  12.7 us
    all_to_all x1, waiting for transfers between devices, shards(): mine = lax.all_to_all(both, 'head', 0, 1, tiled=True)  10 us
    reshape x1, local copies, waits for them, and re-layouts, shards(): wo_cols = stacked[:, n_q + n_kv:].reshape(tok_count, HQ * HD, out_cols).t...  7.08 us
    unnamed x29, local copies, waits for them, and re-layouts  6.45 us
  transfers between devices with their start and end apart: 4, of which 3 were waited for; matrix products, arithmetic and copies ran while one was open for 16% of the time, Pallas kernels for 0%

commit v1 on v0

--- a/solution.py
+++ b/solution.py
@@ -123,7 +123,9 @@
         .transpose(1, 0, 2)
         .reshape(HQ * HD, tok_count * out_cols)
     )
-    gathered = lax.all_gather(tokens, "head", axis=1, tiled=True)
+    gathered = jnp.concatenate(
+        lax.all_to_all(jnp.stack([tokens] * lax.axis_size("head")), "head", 0, 0), axis=1
+    )
     wide = gathered.astype(jnp.float32)
     mean_square = jnp.mean(wide * wide, axis=1, keepdims=True)
     normed = (wide * lax.rsqrt(mean_square + 1e-06)).astype(jnp.bfloat16)

time: 287 us -> 251 us (0.87)
  waiting for transfers between devices: 186 us -> 139 us
  starting transfers between devices: 12.8 us -> 23.2 us
    all_gather x1, waiting for transfers between devices: 146 us -> 103 us  [shards(): stacked = lax.all_gather(flat, 'tok', axis=0, tiled=False)]
    all_gather x1 -> x0, waiting for transfers between devices: 29.1 us -> none  [shards(): gathered = lax.all_gather(tokens, 'head', axis=1, tiled=True)]
    all_to_all x0 -> x1, waiting for transfers between devices: none -> 25.3 us  [shards(): lax.all_to_all(jnp.stack([tokens] * lax.axis_size('head')), 'head', 0, 0)]
    all_to_all x0 -> x1, starting transfers between devices: none -> 10.5 us  [shards(): lax.all_to_all(jnp.stack([tokens] * lax.axis_size('head')), 'head', 0, 0)]
    unnamed x29 -> x33, local copies, waits for them, and re-layouts: 6.45 us -> 6.52 us
where the time goes in v1:
time: 251 us; the launch traced here: 250 us
  waiting for transfers between devices  139 us (55%)
  local copies, waits for them, and re-layouts  53.7 us (21%)
  starting transfers between devices  23.2 us (9%)
  between operations  16.4 us (7%)
  matrix products  9.74 us (4%)
  other arithmetic  8.17 us (3%)
    all_gather x1, waiting for transfers between devices, shards(): stacked = lax.all_gather(flat, 'tok', axis=0, tiled=False)  103 us
    all_to_all x1, waiting for transfers between devices, shards(): lax.all_to_all(jnp.stack([tokens] * lax.axis_size('head')), 'head', 0, 0)  25.3 us
    slice x21, local copies, waits for them, and re-layouts, shards(): wo_cols[k * HD:(k + 1) * HD]  16.9 us
    all_to_all x1, starting transfers between devices, shards(): mine = lax.all_to_all(both, 'head', 0, 1, tiled=True)  12.7 us
    all_to_all x1, waiting for transfers between devices, shards(): mine = lax.all_to_all(both, 'head', 0, 1, tiled=True)  10.7 us
    all_to_all x1, starting transfers between devices, shards(): lax.all_to_all(jnp.stack([tokens] * lax.axis_size('head')), 'head', 0, 0)  10.5 us
    reshape x1, local copies, waits for them, and re-layouts, shards(): wo_cols = stacked[:, n_q + n_kv:].reshape(tok_count, HQ * HD, out_cols).t...  7.08 us
    unnamed x33, local copies, waits for them, and re-layouts  6.52 us
  transfers between devices with their start and end apart: 4, of which 3 were waited for; matrix products, arithmetic and copies ran while one was open for 16% of the time, Pallas kernels for 0%

profile of v1, /device:TPU:1, one launch (start us, length us, event | category | flops | bytes accessed | tf_op | source)
XLA Modules:
  0.0 249.8 jit_solution(5478837662127926145)
XLA Ops:
  7.2 0.8 constant_dynamic-slice_fusion.1
  8.1 0.9 constant_dynamic-slice_fusion.2
  9.1 1.2 copy.63
  10.3 1.0 reshape.350
  11.3 0.7 reshape.378
  12.0 2.8 %stack.8 = bf16[8,512,320]{1,2,0:T(8,128)(2,1)} broadcast(bf16[512,320]{0,1:T(8,128)(2,1)} %param.11), dimensions={1,2} | broadcast | bytes 2949120 | tf_op jit(solution)/shard_map/stack | solution.py:127
  14.8 10.5 %all-to-all-start = ((bf16[8,512,320]{1,2,0:T(8,128)(2,1)}), bf16[8,512,320]{1,2,0:T(8,128)(2,1)S(1)}, u32[]{:S(2)}, u32[]{:S(2)}) async-start(bf16[8,512,320]{1,2,0:T(8,128)(2,1)} %stack.8), calls=%async_computation | async-start | bytes 5242880 | tf_op jit(solution)/shard_map/all_to_all | solution.py:127
  25.3 0.7 fusion.66
  26.4 0.6 dynamic_slice.29
  28.1 0.6 dynamic_slice.25
  30.3 0.7 iota_compare_fusion.6
  31.0 0.7 iota_subtract_fusion
  31.8 25.3 %all-to-all-done = bf16[8,512,320]{1,2,0:T(8,128)(2,1)S(1)} async-done(((bf16[8,512,320]{1,2,0:T(8,128)(2,1)}), bf16[8,512,320]{1,2,0:T(8,128)(2,1)S(1)}, u32[]{:S(2)}, u32[]{:S(2)}) %all-to-all-start) | async-done | bytes 2621472 | tf_op jit(solution)/shard_map/all_to_all | solution.py:127
  57.1 0.6 fusion
  57.8 2.1 fusion.1
  59.8 102.5 %all-gather.7.cloned.1.call-done = bf16[64,1,28160]{2,1,0:T(2,128)(2,1)} async-done(((bf16[1,1,28160]{2,1,0:T(2,128)(2,1)}), bf16[64,1,28160]{2,1,0:T(2,128)(2,1)}) %all-gather.7.cloned.1.call-update) | async-done | bytes 3604496 | tf_op jit(solution)/shard_map/all_gather | solution.py:114
  162.4 3.5 %copy.98 = bf16[64,1,28160]{2,0,1:T(8,128)(2,1)S(1)} copy(bf16[64,1,28160]{2,1,0:T(2,128)(2,1)} %all-gather.7.cloned.1.call-done) | data formatting | bytes 7208960
  165.9 1.9 fusion.75
  167.8 1.2 reshape.352
  169.0 4.1 %reshape.351 = bf16[2560,320]{1,0:T(8,128)(2,1)} reshape(bf16[64,12800]{1,0:T(8,128)(2,1)} %get-tuple-element.16) | data formatting | bytes 3276800 | tf_op jit(solution)/shard_map/reshape | solution.py:118
  173.2 2.7 %fusion.84 = f32[512,320]{0,1:T(8,128)S(1)} fusion(bf16[512,2560]{0,1:T(8,128)(2,1)S(1)} %bitcast.120, bf16[2560,320]{1,0:T(8,128)(2,1)} %reshape.351), kind=kOutput, calls=%fused_computation.149 | convolution fusion | flops 838860800 | bytes 4915200 | tf_op jit(solution)/shard_map/dot_general | solution.py:132
  175.9 0.6 fusion.85
  176.5 1.1 copy.64
  177.7 12.7 %all-to-all-start.1 = ((f32[8,64,384]{2,1,0:T(8,128)}), f32[8,64,384]{2,1,0:T(8,128)S(1)}, u32[]{:S(2)}, u32[]{:S(2)}) async-start(f32[8,64,384]{2,1,0:T(8,128)} %bitcast.9), calls=%async_computation.1 | async-start | bytes 1572864 | tf_op jit(solution)/shard_map/all_to_all | solution.py:135
  190.5 0.6 gather_fusion
  191.1 0.7 add_add_fusion
  191.9 10.7 %all-to-all-done.1 = f32[8,64,384]{2,1,0:T(8,128)S(1)} async-done(((f32[8,64,384]{2,1,0:T(8,128)}), f32[8,64,384]{2,1,0:T(8,128)S(1)}, u32[]{:S(2)}, u32[]{:S(2)}) %all-to-all-start.1) | async-done | bytes 786464 | tf_op jit(solution)/shard_map/all_to_all | solution.py:135
  203.0 0.3 convolution_convert_fusion.8
  203.3 0.5 copy.65
  203.8 0.4 reshape.353
  204.7 0.3 convolution_convert_fusion.9
  205.0 1.0 fusion.32
  206.4 0.4 fusion.80
  206.8 0.5 fusion.79
  207.3 0.4 fusion.22
  207.8 0.3 fusion.46
  208.1 0.4 fusion.81
  208.5 0.7 copy.91
  209.6 2.9 %copy.73 = bf16[64,12800]{0,1:T(8,128)(2,1)} copy(bf16[64,12800]{1,0:T(8,128)(2,1)S(1)} %copy-done.3) | data formatting | bytes 3276800 | tf_op jit(solution)/shard_map/slice | solution.py:121
  212.5 7.1 %reshape.358 = bf16[64,2560,5]{0,2,1:T(8,128)(2,1)} reshape(bf16[64,12800]{0,1:T(8,128)(2,1)} %copy.73) | data formatting | bytes 3276800 | tf_op jit(solution)/shard_map/reshape | solution.py:122
  219.6 5.0 %fusion.74 = (bf16[256,64,5]{1,2,0:T(8,128)(2,1)}, bf16[256,64,5]{1,2,0:T(8,128)(2,1)}, bf16[256,64,5]{1,2,0:T(8,128)(2,1)}, bf16[256,64,5]{1,2,0:T(8,128)(2,1)}...) fusion(bf16[2560,64,5]{1,2,0:T(8,128)(2,1)} %bitcast.117), kind=kLoop, calls=%fused_computation.141 | loop fusion | bytes 3276800 | tf_op jit(solution)/shard_map/slice | solution.py:171
  224.5 1.5 copy.83
  226.0 0.7 slice.181
  226.8 1.5 copy.82
  228.2 0.7 slice.178
  229.0 1.5 copy.81
  230.5 0.7 slice.175
  231.2 1.5 copy.80
  232.7 0.7 slice.172
  233.5 0.4 copy.79
  234.0 0.4 copy.78
  234.5 0.4 copy.77
  235.1 0.4 copy.76
  235.6 0.4 copy.75
  236.1 0.4 copy.74
  236.7 0.6 gather_fusion.1
  237.3 0.9 broadcast_select_fusion
  238.2 1.4 fusion.76
  239.6 0.4 fusion.19
  240.0 0.4 fusion.18
  240.7 0.3 fusion.14
  241.0 0.3 fusion.12
  241.6 0.3 fusion.8
  241.9 1.0 fusion.6
  (82 shorter events, 4.8 us)
Async XLA Ops:
  7.2 183.3 %copy-start = (bf16[4,2,128,256]{3,2,1,0:T(8,128)(2,1)S(1)}, bf16[4,2,128,256]{3,2,1,0:T(8,128)(2,1)}, u32[]{:S(2)}) copy-start(bf16[4,2,128,256]{3,2,1,0:T(8,128)(2,1)} %param.15) | copy-start | bytes 1572868
  7.2 155.2 %all-gather.7.cloned.1.call-start = ((), (), s32[]{:S(2)}) async-start(), calls=%async_computation.3 | async-start | bytes 7321600 | tf_op jit(solution)/shard_map/all_gather | solution.py:114
  14.8 11.6 %copy-start.12 = (s32[8]{0:T(128)S(1)}, s32[8]{0:T(128)}, u32[]{:S(2)}) copy-start(s32[8]{0:T(128)} %param.19) | copy-start | bytes 100
  14.8 13.4 %copy-start.13 = (s32[8]{0:T(128)S(1)}, s32[8]{0:T(128)}, u32[]{:S(2)}) copy-start(s32[8]{0:T(128)} %param.18) | copy-start | bytes 100
  14.8 15.3 %copy-start.11 = (s32[8,4]{0,1:T(4,128)S(1)}, s32[8,4]{0,1:T(4,128)}, u32[]{:S(2)}) copy-start(s32[8,4]{0,1:T(4,128)} %param.16) | copy-start | bytes 388
  14.8 42.3 %all-to-all-start = ((bf16[8,512,320]{1,2,0:T(8,128)(2,1)}), bf16[8,512,320]{1,2,0:T(8,128)(2,1)S(1)}, u32[]{:S(2)}, u32[]{:S(2)}) async-start(bf16[8,512,320]{1,2,0:T(8,128)(2,1)} %stack.8), calls=%async_computation | async-start | bytes 5242880 | tf_op jit(solution)/shard_map/all_to_all | solution.py:127
  167.8 5.4 %copy-start.2 = (bf16[8,512,320]{1,2,0:T(8,128)(2,1)S(1)}, bf16[8,512,320]{1,2,0:T(8,128)(2,1)}, u32[]{:S(2)}) copy-start(bf16[8,512,320]{1,2,0:T(8,128)(2,1)} %fusion.1) | copy-start | bytes 7864324
  173.2 2.7 %copy-start.5 = (bf16[2560,64]{1,0:T(8,128)(2,1)S(1)}, bf16[2560,64]{1,0:T(8,128)(2,1)}, u32[]{:S(2)}) copy-start(bf16[2560,64]{1,0:T(8,128)(2,1)} %reshape.352) | copy-start | bytes 983044
  177.7 24.9 %all-to-all-start.1 = ((f32[8,64,384]{2,1,0:T(8,128)}), f32[8,64,384]{2,1,0:T(8,128)S(1)}, u32[]{:S(2)}, u32[]{:S(2)}) async-start(f32[8,64,384]{2,1,0:T(8,128)} %bitcast.9), calls=%async_computation.1 | async-start | bytes 1572864 | tf_op jit(solution)/shard_map/all_to_all | solution.py:135
  190.4 47.8 %all-gather.5.cloned.1.call-start = ((), (), s32[]{:S(2)}) async-start(), calls=%async_computation.2 | async-start | bytes 2949120 | tf_op jit(solution)/shard_map/all_gather | solution.py:164
  208.1 1.5 copy-start.3
  234.4 2.2 copy-start.6
  238.2 2.2 copy-start.4
  240.0 1.0 copy-start.10
  240.3 0.9 copy-start.9
  240.6 0.9 copy-start.8
  240.9 1.0 copy-start.7
  241.0 2.0 copy-start.1
Sparse Core Ops, SparseCore 0:
  12.1 150.2 all-gather.6
  209.4 27.9 all-gather.4
